TPU v7x, 256 devices: a whole 4x4x8 slice. The times are simulated.
256 devices in a mesh: stn: 64 (over y, z, core), sec: 4 (over x).
Axes of the slice: x: 4, y: 4, z: 8, core: 2. Of those that a mesh axis runs over, the one named last changes fastest.
Arguments:
- voltages: bfloat16 [2, 1024, 569344], P(None, ('stn', 'sec')), may hold values from -6 to 6
- fir_taps: float32 [12, 4096], replicated, may hold values from -1.75 to 1.75
- cor_channels: int32 [256], replicated, may hold values from 0 to 4095, as said below
- beam_channels: int32 [256], replicated, may hold values from 1 to 4094, as said below
- cor_gain: float32 [256], replicated, as said below
- beam_gain: float32 [256], replicated, as said below
- beam_stations: int32 [16, 512], replicated, may hold values from 0 to 511
- beam_codes: int32 [16, 512], replicated, may hold values from 0 to 255
Outputs:
- visibilities: bfloat16 [256, 2, 1024, 1024], P(('stn', 'sec'))
- beams: bfloat16 [256, 16, 2, 256], P(('stn', 'sec'))
Inputs may be any that keep to these rules, and one draw needn't show every extreme that they name: cor_channels and beam_channels together are 512 distinct transform channels. None of beam_channels appears in cor_channels. `cor_gain`: positive. `beam_gain`: positive.
All inputs are finite; a program needn't handle non-finite values.
Results may differ from a plain program's by a relative error of at most 0.0085.
Values may be sent and summed in bfloat16 or wider, within the bound.
No kernel may reach another device: no remote copies, remote signals or barrier semaphores. Data moves between devices by JAX's collectives and lax.ppermute only.
A program may use at most 128 MiB of HBM per device.

v0:
```python
import math
import jax
import jax.numpy as jnp
from jax import lax
from jax.sharding import PartitionSpec as P

STATIONS = 512
epsilon = 1e-05


def make_tables(channel_of, points):
    sample_index = jnp.arange(points, dtype=jnp.int32)
    phase_turns = channel_of[:, None] * sample_index[None, :] % points
    phase_angle = phase_turns.astype(jnp.float32) * (2.0 * math.pi / points)
    table_scale = 1.0 / math.sqrt(points)
    cos_table = (jnp.cos(phase_angle) * table_scale).astype(jnp.bfloat16)
    sin_table = (jnp.sin(phase_angle) * table_scale).astype(jnp.bfloat16)
    return (cos_table, sin_table)


def make_weights(beam_stations, beam_codes, stations):
    station_ids = jnp.arange(stations, dtype=jnp.int32)
    onehot = (beam_stations[:, :, None] == station_ids[None, None, :]).astype(jnp.float32)
    amplitude = (1 + beam_codes // 64).astype(jnp.float32)
    phase_angle = (beam_codes % 64).astype(jnp.float32) * (2.0 * math.pi / 64.0)
    weight_re = jnp.einsum("bk,bks->bs", amplitude * jnp.cos(phase_angle), onehot)
    weight_im = jnp.einsum("bk,bks->bs", amplitude * jnp.sin(phase_angle), onehot)
    return (weight_re.astype(jnp.bfloat16), weight_im.astype(jnp.bfloat16))


def polyphase(in_block, fir_taps, spectra):
    tap_count, points = fir_taps.shape
    framed = in_block.reshape(in_block.shape[0], in_block.shape[1], -1, points)
    summed = jnp.zeros((framed.shape[0], framed.shape[1], spectra, points), jnp.float32)
    for tap_index in range(tap_count):
        summed = summed + fir_taps[tap_index] * framed[
            :, :, tap_index : tap_index + spectra, :
        ].astype(jnp.float32)
    return summed.astype(jnp.bfloat16)


def contract(left_rows, right_rows):
    contract_dims = (((1,), (1,)), ((), ()))
    return lax.dot_general(left_rows, right_rows, contract_dims, preferred_element_type=jnp.float32)


def spectrum(filtered, cos_table, sin_table, slot_gain):
    inputs_here, spectra, points = (filtered.shape[1], filtered.shape[2], filtered.shape[3])
    real_rows = filtered[0].reshape(inputs_here * spectra, points)
    imag_rows = filtered[1].reshape(inputs_here * spectra, points)
    spec_re = contract(cos_table, real_rows) + contract(sin_table, imag_rows)
    spec_im = contract(cos_table, imag_rows) - contract(sin_table, real_rows)
    combined = jnp.concatenate(
        [spec_re.reshape(-1, inputs_here, spectra), spec_im.reshape(-1, inputs_here, spectra)],
        axis=2,
    )
    return (combined * slot_gain[:, None, None]).astype(jnp.bfloat16)


def form_beams(beam_data, weight_re, weight_im):
    spectra = beam_data.shape[2] // 2
    samples = beam_data.reshape(beam_data.shape[0], -1, 2, beam_data.shape[2])
    with_re = jnp.einsum("bs,jspt->jbpt", weight_re, samples, preferred_element_type=jnp.float32)
    with_im = jnp.einsum("bs,jspt->jbpt", weight_im, samples, preferred_element_type=jnp.float32)
    out_re = with_re[..., :spectra] - with_im[..., spectra:]
    out_im = with_re[..., spectra:] + with_im[..., :spectra]
    return jnp.concatenate([out_re, out_im], axis=3)


def per_device(
    voltages, fir_taps, cor_channels, beam_channels, cor_gain, beam_gain, beam_stations, beam_codes
):
    tap_count, points = fir_taps.shape
    stn_count = lax.axis_size("stn")
    sec_count = lax.axis_size("sec")
    device_count = stn_count * sec_count
    inputs_here = voltages.shape[1]
    spectra = voltages.shape[2] // points - tap_count + 1
    filtered = polyphase(voltages, fir_taps, spectra)
    channel_of = jnp.concatenate([cor_channels, beam_channels])
    slot_gain = jnp.concatenate([cor_gain, beam_gain])
    cos_table, sin_table = make_tables(channel_of, points)
    weight_re, weight_im = make_weights(beam_stations, beam_codes, STATIONS)
    spectra_all = spectrum(filtered, cos_table, sin_table, slot_gain)
    outgoing = spectra_all.reshape(2, stn_count, sec_count, 1, 1, inputs_here, 2 * spectra)
    turned = lax.all_to_all(
        lax.all_to_all(outgoing, "stn", split_axis=1, concat_axis=3, tiled=True),
        "sec",
        split_axis=2,
        concat_axis=4,
        tiled=True,
    )
    received = turned.reshape(2, device_count * inputs_here, 2 * spectra)
    cor_data = received[0]
    beam_data = received[1:2]
    swapped = jnp.concatenate([cor_data[:, spectra:], -cor_data[:, :spectra]], axis=1)
    vis_re = contract(cor_data, cor_data) / spectra
    vis_im = contract(swapped, cor_data) / spectra
    visibilities = jnp.stack([vis_re, vis_im])[None].astype(jnp.bfloat16)
    raw_beams = form_beams(beam_data, weight_re, weight_im)
    local_power = jnp.sum(raw_beams * raw_beams, axis=(0, 2, 3))
    summed_power = lax.psum(local_power, ("stn", "sec"))
    beam_power = summed_power / (device_count * raw_beams.shape[2] * raw_beams.shape[3])
    beams = (raw_beams * lax.rsqrt(beam_power + epsilon)[None, :, None, None]).astype(jnp.bfloat16)
    return (visibilities, beams)


def solution(mesh):
    in_specs = (P(None, ("stn", "sec"), None), P(), P(), P(), P(), P(), P(), P())
    out_specs = (P(("stn", "sec"), None, None, None), P(("stn", "sec"), None, None, None))
    return jax.shard_map(
        per_device, mesh=mesh, in_specs=in_specs, out_specs=out_specs, check_vma=False
    )
```

profile of v0, /device:TPU:1, one launch (start us, length us, event | category | flops | bytes accessed | tf_op | source)
XLA Modules:
  0.0 348.5 jit_solution(4968068274849040461)
XLA Ops:
  0.6 1.8 fusion.60
  2.5 14.5 %reshape.175 = bf16[2,4,139,4096]{3,2,1,0:T(8,128)(2,1)} reshape(bf16[2,4,569344]{2,1,0:T(4,128)(2,1)} %param.8) | data formatting | bytes 18219008 | tf_op jit(solution)/shard_map/reshape | solution.py:33
  17.0 52.5 %add_convert_fusion = bf16[2,4,128,4096]{3,2,1,0:T(8,128)(2,1)} fusion(bf16[2,4,139,4096]{3,2,1,0:T(8,128)(2,1)} %reshape.175, f32[4096]{0:T(1024)S(1)} %bitcast.81, f32[4096]{0:T(1024)S(1)} %bitcast.82, f32[4096]{0:T(1024)S(1)} %bitcast.72, f32[4096]{0:T(1024)S(1)} %bitcast.73, f32[4096]{0:T(1024)S(1)} %bitcast.74, f32[4096]{0:T(1024)S(1)} %bitcast.75, ...), kind=kLoop, calls=%fused_computation.3 | loop fusion | flops 150994944 | bytes 109248512 | tf_op jit(solution)/shard_map/convert_element_type | solution.py:39
  69.5 4.0 %fusion.57 = (bf16[1,4,128,4096]{3,2,1,0:T(8,128)(2,1)S(1)}, bf16[1,4,128,4096]{3,2,1,0:T(8,128)(2,1)S(1)}) fusion(bf16[2,4,128,4096]{3,2,1,0:T(8,128)(2,1)} %add_convert_fusion), kind=kLoop, calls=%fused_computation.88 | loop fusion | bytes 16777216 | tf_op jit(solution)/shard_map/slice | solution.py:49
  73.6 31.8 %fusion.11 = f32[512,512]{1,0:T(8,128)S(1)} fusion(bf16[512,4096]{1,0:T(8,128)(2,1)S(1)} %bitcast.67, s32[512]{0:T(512)S(1)} %pad_add_fusion), kind=kOutput, calls=%fused_computation.21 | convolution fusion | flops 2181038080 | bytes 5244928 | tf_op jit(solution)/shard_map/dot_general | solution.py:44
  105.4 32.4 %fusion.10 = f32[512,512]{1,0:T(8,128)} fusion(bf16[512,4096]{1,0:T(8,128)(2,1)S(1)} %bitcast.69, s32[512]{0:T(512)S(1)} %pad_add_fusion), kind=kOutput, calls=%fused_computation.20 | convolution fusion | flops 2181038080 | bytes 5244928 | tf_op jit(solution)/shard_map/dot_general | solution.py:44
  137.7 32.1 %fusion.17 = f32[512,512]{1,0:T(8,128)S(1)} fusion(f32[512,512]{1,0:T(8,128)S(1)} %fusion.11, bf16[512,4096]{1,0:T(8,128)(2,1)S(1)} %bitcast.70, s32[512]{0:T(512)S(1)} %pad_add_fusion), kind=kOutput, calls=%fused_computation.29 | convolution fusion | flops 2181300224 | bytes 6293504 | tf_op jit(solution)/shard_map/dot_general | solution.py:44
  169.8 0.4 concatenate.56
  170.2 34.4 %fusion.18 = f32[512,512]{1,0:T(8,128)S(1)} fusion(f32[512,512]{1,0:T(8,128)} %fusion.10, bf16[512,4096]{1,0:T(8,128)(2,1)} %bitcast.68, s32[512]{0:T(512)S(1)} %pad_add_fusion), kind=kOutput, calls=%fused_computation.30 | convolution fusion | flops 2181300224 | bytes 6293504 | tf_op jit(solution)/shard_map/dot_general | solution.py:44
  204.7 0.4 concatenate.57
  205.1 0.1 concatenate.59
  205.4 0.7 fusion.14
  206.1 41.5 %all_to_all.33 = bf16[2,64,4,1,1,4,256]{6,5,2,0,4,3,1:T(4,128)(2,1)S(1)} all-to-all(bf16[2,64,4,1,1,4,256]{6,5,2,0,4,3,1:T(4,128)(2,1)S(1)} %fusion.14), channel_id=1, replica_groups=mesh['stn'=64,'sec'=4] {'stn'}, dimensions={1} | all-to-all | bytes 2097152 | tf_op jit(solution)/shard_map/all_to_all | solution.py:87
  247.6 1.4 copy.38
  249.0 4.0 %all-to-all-start.1 = ((bf16[2,1,4,64,1,4,256]{6,5,3,0,4,1,2:T(4,128)(2,1)}), bf16[2,1,4,64,1,4,256]{6,5,3,0,4,1,2:T(4,128)(2,1)S(1)}, u32[]{:S(2)}, u32[]{:S(2)}) async-start(bf16[2,1,4,64,1,4,256]{6,5,3,0,4,1,2:T(4,128)(2,1)} %copy.38), calls=%async_computation.1 | async-start | bytes 2097152 | tf_op jit(solution)/shard_map/all_to_all | solution.py:86
  253.0 0.2 multiply_bitcast_fusion.1
  253.2 3.2 fusion
  256.4 3.2 fusion.1
  259.6 8.3 %all-to-all-done.1 = bf16[2,1,4,64,1,4,256]{6,5,3,0,4,1,2:T(4,128)(2,1)S(1)} async-done(((bf16[2,1,4,64,1,4,256]{6,5,3,0,4,1,2:T(4,128)(2,1)}), bf16[2,1,4,64,1,4,256]{6,5,3,0,4,1,2:T(4,128)(2,1)S(1)}, u32[]{:S(2)}, u32[]{:S(2)}) %all-to-all-start.1) | async-done | bytes 1048608 | tf_op jit(solution)/shard_map/all_to_all | solution.py:86
  267.9 0.4 fusion.58
  268.3 0.2 copy.40
  268.5 0.3 reshape.176
  268.7 0.2 convolution_bitcast_fusion
  268.9 0.2 convolution_bitcast_fusion.1
  269.1 0.2 copy.39
  269.3 0.1 squeeze.3
  269.5 0.1 multiply_reduce_fusion
  269.6 0.7 fusion.15
  270.4 74.1 %psum.7 = f32[16]{0:T(128)S(1)} all-reduce(f32[16]{0:T(128)S(1)} %multiply_reduce_fusion), channel_id=1, replica_groups=mesh['stn'=64,'sec'=4] {'stn','sec'}, use_global_device_ids=true, to_apply=%region_1.2 | all-reduce | flops 16 | bytes 128 | tf_op jit(solution)/shard_map/psum | solution.py:102
  344.5 0.6 copy.43
  345.1 0.7 fusion.16
  345.9 2.4 pad_maximum_fusion
  (22 shorter events, 0.4 us)
Async XLA Ops:
  69.5 4.0 %copy-start.4 = (s32[256]{0:T(256)S(1)}, s32[256]{0:T(256)}, u32[]{:S(2)}) copy-start(s32[256]{0:T(256)} %param.11) | copy-start | bytes 3076
  69.5 4.0 %copy-start.5 = (s32[256]{0:T(256)S(1)}, s32[256]{0:T(256)}, u32[]{:S(2)}) copy-start(s32[256]{0:T(256)} %param.10) | copy-start | bytes 3076
  73.5 31.8 %copy-start = (bf16[1,4,128,4096]{3,2,1,0:T(8,128)(2,1)}, bf16[1,4,128,4096]{3,2,1,0:T(8,128)(2,1)S(1)}, u32[]{:S(2)}) copy-start(bf16[1,4,128,4096]{3,2,1,0:T(8,128)(2,1)S(1)} %get-tuple-element.12) | copy-start | bytes 12582916
  170.2 34.8 %copy-start.2 = (f32[256]{0:T(256)S(1)}, f32[256]{0:T(256)}, u32[]{:S(2)}) copy-start(f32[256]{0:T(256)} %param.12) | copy-start | bytes 3076
  170.2 35.0 %copy-start.3 = (f32[256]{0:T(256)S(1)}, f32[256]{0:T(256)}, u32[]{:S(2)}) copy-start(f32[256]{0:T(256)} %param.13) | copy-start | bytes 3076
  204.7 48.4 %copy-start.1 = (s32[16,512]{1,0:T(8,128)S(1)}, s32[16,512]{1,0:T(8,128)}, u32[]{:S(2)}) copy-start(s32[16,512]{1,0:T(8,128)} %param.15) | copy-start | bytes 98308
  204.7 48.5 %copy-start.6 = (s32[16,512]{1,0:T(8,128)S(1)}, s32[16,512]{1,0:T(8,128)}, u32[]{:S(2)}) copy-start(s32[16,512]{1,0:T(8,128)} %param.14) | copy-start | bytes 98308
  249.0 18.9 %all-to-all-start.1 = ((bf16[2,1,4,64,1,4,256]{6,5,3,0,4,1,2:T(4,128)(2,1)}), bf16[2,1,4,64,1,4,256]{6,5,3,0,4,1,2:T(4,128)(2,1)S(1)}, u32[]{:S(2)}, u32[]{:S(2)}) async-start(bf16[2,1,4,64,1,4,256]{6,5,3,0,4,1,2:T(4,128)(2,1)} %copy.38), calls=%async_computation.1 | async-start | bytes 2097152 | tf_op jit(solution)/shard_map/all_to_all | solution.py:86
where the time goes:
time: 352 us; the launch traced here: 348 us
  matrix products  139 us (39%)
  blocking collectives  116 us (33%)
  other arithmetic  56.1 us (16%)
  local copies, waits for them, and re-layouts  24.4 us (7%)
  waiting for transfers between devices  8.26 us (2%)
  starting transfers between devices  4.03 us (1%)
    dot_general x6, matrix products, contract(): lax.dot_general(left_rows, right_rows, contract_dims, preferred_element_t...  132 us
    psum x1, blocking collectives, per_device(): summed_power = lax.psum(local_power, ('stn', 'sec'))  74.1 us
    convert_element_type x1, other arithmetic, polyphase(): return summed.astype(jnp.bfloat16)  52.5 us
    all_to_all x1, blocking collectives, per_device(): lax.all_to_all(outgoing, 'stn', split_axis=1, concat_axis=3, tiled=True)  41.5 us
    reshape x1, local copies, waits for them, and re-layouts, polyphase(): framed = in_block.reshape(in_block.shape[0], in_block.shape[1], -1, points)  14.5 us
    all_to_all x1, waiting for transfers between devices, per_device(): lax.all_to_all(lax.all_to_all(outgoing, 'stn', split_axis=1, concat_axis=...  8.26 us
  transfers between devices with their start and end apart: 1, of which 1 were waited for; matrix products, arithmetic and copies ran while one was open for 2% of the time, Pallas kernels for 0%

commit v1 on v0

--- a/solution.py
+++ b/solution.py
@@ -99,7 +99,7 @@
     visibilities = jnp.stack([vis_re, vis_im])[None].astype(jnp.bfloat16)
     raw_beams = form_beams(beam_data, weight_re, weight_im)
     local_power = jnp.sum(raw_beams * raw_beams, axis=(0, 2, 3))
-    summed_power = lax.psum(local_power, ("stn", "sec"))
+    summed_power = lax.psum(lax.psum(local_power, "sec"), "stn")
     beam_power = summed_power / (device_count * raw_beams.shape[2] * raw_beams.shape[3])
     beams = (raw_beams * lax.rsqrt(beam_power + epsilon)[None, :, None, None]).astype(jnp.bfloat16)
     return (visibilities, beams)

time: 352 us -> 411 us (1.17)
  blocking collectives: 116 us -> 175 us
    psum x1 -> x2, blocking collectives: 74.1 us -> 133 us  [per_device(): summed_power = lax.psum(lax.psum(local_power, 'sec'), 'stn')]
where the time goes in v1:
time: 411 us; the launch traced here: 408 us
  blocking collectives  175 us (43%)
  matrix products  139 us (34%)
  other arithmetic  56 us (14%)
  local copies, waits for them, and re-layouts  24.4 us (6%)
  waiting for transfers between devices  8.26 us (2%)
    psum x2, blocking collectives, per_device(): summed_power = lax.psum(lax.psum(local_power, 'sec'), 'stn')  133 us
    dot_general x6, matrix products, contract(): lax.dot_general(left_rows, right_rows, contract_dims, preferred_element_t...  132 us
    convert_element_type x1, other arithmetic, polyphase(): return summed.astype(jnp.bfloat16)  52.4 us
    all_to_all x1, blocking collectives, per_device(): lax.all_to_all(outgoing, 'stn', split_axis=1, concat_axis=3, tiled=True)  41.5 us
    reshape x1, local copies, waits for them, and re-layouts, polyphase(): framed = in_block.reshape(in_block.shape[0], in_block.shape[1], -1, points)  14.5 us
    all_to_all x1, waiting for transfers between devices, per_device(): lax.all_to_all(lax.all_to_all(outgoing, 'stn', split_axis=1, concat_axis=...  8.26 us
  transfers between devices with their start and end apart: 1, of which 1 were waited for; matrix products, arithmetic and copies ran while one was open for 2% of the time, Pallas kernels for 0%

profile of v1, /device:TPU:1, one launch (start us, length us, event | category | flops | bytes accessed | tf_op | source)
XLA Modules:
  0.0 407.8 jit_solution(10272800225670803010)
XLA Ops:
  0.6 1.8 fusion.60
  2.5 14.5 %reshape.175 = bf16[2,4,139,4096]{3,2,1,0:T(8,128)(2,1)} reshape(bf16[2,4,569344]{2,1,0:T(4,128)(2,1)} %param.8) | data formatting | bytes 18219008 | tf_op jit(solution)/shard_map/reshape | solution.py:33
  17.0 52.4 %add_convert_fusion = bf16[2,4,128,4096]{3,2,1,0:T(8,128)(2,1)} fusion(bf16[2,4,139,4096]{3,2,1,0:T(8,128)(2,1)} %reshape.175, f32[4096]{0:T(1024)S(1)} %bitcast.81, f32[4096]{0:T(1024)S(1)} %bitcast.82, f32[4096]{0:T(1024)S(1)} %bitcast.72, f32[4096]{0:T(1024)S(1)} %bitcast.73, f32[4096]{0:T(1024)S(1)} %bitcast.74, f32[4096]{0:T(1024)S(1)} %bitcast.75, ...), kind=kLoop, calls=%fused_computation.3 | loop fusion | flops 150994944 | bytes 109248512 | tf_op jit(solution)/shard_map/convert_element_type | solution.py:39
  69.4 4.0 fusion.57
  73.4 31.8 %fusion.11 = f32[512,512]{1,0:T(8,128)S(1)} fusion(bf16[512,4096]{1,0:T(8,128)(2,1)S(1)} %bitcast.67, s32[512]{0:T(512)S(1)} %pad_add_fusion), kind=kOutput, calls=%fused_computation.21 | convolution fusion | flops 2181038080 | bytes 5244928 | tf_op jit(solution)/shard_map/dot_general | solution.py:44
  105.3 32.4 %fusion.10 = f32[512,512]{1,0:T(8,128)} fusion(bf16[512,4096]{1,0:T(8,128)(2,1)S(1)} %bitcast.69, s32[512]{0:T(512)S(1)} %pad_add_fusion), kind=kOutput, calls=%fused_computation.20 | convolution fusion | flops 2181038080 | bytes 5244928 | tf_op jit(solution)/shard_map/dot_general | solution.py:44
  137.6 32.1 %fusion.17 = f32[512,512]{1,0:T(8,128)S(1)} fusion(f32[512,512]{1,0:T(8,128)S(1)} %fusion.11, bf16[512,4096]{1,0:T(8,128)(2,1)S(1)} %bitcast.70, s32[512]{0:T(512)S(1)} %pad_add_fusion), kind=kOutput, calls=%fused_computation.29 | convolution fusion | flops 2181300224 | bytes 6293504 | tf_op jit(solution)/shard_map/dot_general | solution.py:44
  169.7 0.4 concatenate.56
  170.1 34.4 %fusion.18 = f32[512,512]{1,0:T(8,128)S(1)} fusion(f32[512,512]{1,0:T(8,128)} %fusion.10, bf16[512,4096]{1,0:T(8,128)(2,1)} %bitcast.68, s32[512]{0:T(512)S(1)} %pad_add_fusion), kind=kOutput, calls=%fused_computation.30 | convolution fusion | flops 2181300224 | bytes 6293504 | tf_op jit(solution)/shard_map/dot_general | solution.py:44
  204.6 0.4 concatenate.57
  205.3 0.7 fusion.14
  206.0 41.5 %all_to_all.33 = bf16[2,64,4,1,1,4,256]{6,5,2,0,4,3,1:T(4,128)(2,1)S(1)} all-to-all(bf16[2,64,4,1,1,4,256]{6,5,2,0,4,3,1:T(4,128)(2,1)S(1)} %fusion.14), channel_id=1, replica_groups=mesh['stn'=64,'sec'=4] {'stn'}, dimensions={1} | all-to-all | bytes 2097152 | tf_op jit(solution)/shard_map/all_to_all | solution.py:87
  247.5 1.4 copy.38
  248.9 4.0 all-to-all-start.1
  252.9 0.2 multiply_bitcast_fusion.1
  253.1 3.2 fusion
  256.3 3.2 fusion.1
  259.5 8.3 %all-to-all-done.1 = bf16[2,1,4,64,1,4,256]{6,5,3,0,4,1,2:T(4,128)(2,1)S(1)} async-done(((bf16[2,1,4,64,1,4,256]{6,5,3,0,4,1,2:T(4,128)(2,1)}), bf16[2,1,4,64,1,4,256]{6,5,3,0,4,1,2:T(4,128)(2,1)S(1)}, u32[]{:S(2)}, u32[]{:S(2)}) %all-to-all-start.1) | async-done | bytes 1048608 | tf_op jit(solution)/shard_map/all_to_all | solution.py:86
  267.8 0.4 fusion.58
  268.2 0.2 copy.40
  268.4 0.3 reshape.176
  268.6 0.2 convolution_bitcast_fusion
  268.8 0.2 convolution_bitcast_fusion.1
  269.0 0.1 multiply_reduce_fusion
  269.1 6.9 %psum.14 = f32[16]{0:T(128)S(1)} all-reduce(f32[16]{0:T(128)S(1)} %multiply_reduce_fusion), channel_id=1, replica_groups=mesh['stn'=64,'sec'=4] {'sec'}, use_global_device_ids=true, to_apply=%region_1.2 | all-reduce | flops 16 | bytes 128 | tf_op jit(solution)/shard_map/psum | solution.py:102
  276.0 0.2 copy.39
  276.2 0.1 squeeze.3
  276.4 0.7 fusion.15
  277.2 126.6 %psum.15 = f32[16]{0:T(128)S(1)} all-reduce(f32[16]{0:T(128)S(1)} %psum.14), channel_id=1, replica_groups=mesh['stn'=64,'sec'=4] {'stn'}, use_global_device_ids=true, to_apply=%region_2.3 | all-reduce | flops 16 | bytes 128 | tf_op jit(solution)/shard_map/psum | solution.py:102
  403.8 0.6 copy.43
  404.5 0.7 fusion.16
  405.2 2.4 pad_maximum_fusion
  (23 shorter events, 0.5 us)
Async XLA Ops:
  69.4 4.0 copy-start.4
  69.4 4.0 copy-start.5
  73.4 31.8 %copy-start = (bf16[1,4,128,4096]{3,2,1,0:T(8,128)(2,1)}, bf16[1,4,128,4096]{3,2,1,0:T(8,128)(2,1)S(1)}, u32[]{:S(2)}) copy-start(bf16[1,4,128,4096]{3,2,1,0:T(8,128)(2,1)S(1)} %get-tuple-element.12) | copy-start | bytes 12582916
  170.1 34.8 %copy-start.2 = (f32[256]{0:T(256)S(1)}, f32[256]{0:T(256)}, u32[]{:S(2)}) copy-start(f32[256]{0:T(256)} %param.12) | copy-start | bytes 3076
  170.1 35.0 %copy-start.3 = (f32[256]{0:T(256)S(1)}, f32[256]{0:T(256)}, u32[]{:S(2)}) copy-start(f32[256]{0:T(256)} %param.13) | copy-start | bytes 3076
  204.5 48.4 %copy-start.1 = (s32[16,512]{1,0:T(8,128)S(1)}, s32[16,512]{1,0:T(8,128)}, u32[]{:S(2)}) copy-start(s32[16,512]{1,0:T(8,128)} %param.15) | copy-start | bytes 98308
  204.6 48.5 %copy-start.6 = (s32[16,512]{1,0:T(8,128)S(1)}, s32[16,512]{1,0:T(8,128)}, u32[]{:S(2)}) copy-start(s32[16,512]{1,0:T(8,128)} %param.14) | copy-start | bytes 98308
  248.9 18.9 %all-to-all-start.1 = ((bf16[2,1,4,64,1,4,256]{6,5,3,0,4,1,2:T(4,128)(2,1)}), bf16[2,1,4,64,1,4,256]{6,5,3,0,4,1,2:T(4,128)(2,1)S(1)}, u32[]{:S(2)}, u32[]{:S(2)}) async-start(bf16[2,1,4,64,1,4,256]{6,5,3,0,4,1,2:T(4,128)(2,1)} %copy.38), calls=%async_computation.1 | async-start | bytes 2097152 | tf_op jit(solution)/shard_map/all_to_all | solution.py:86
